TPU v7x, 32 devices: a whole 2x2x4 slice. The times are simulated.
32 devices in a mesh: dp: 8 (over z, y), tensor: 4 (over x, core).
Axes of the slice: x: 2, y: 2, z: 4, core: 2. Of those that a mesh axis runs over, the one named last changes fastest.
Arguments:
- pre_hidden: bfloat16 [8192, 2048], P(('dp', 'tensor')), may hold values from -6 to 6
- dec_hidden: bfloat16 [16, 2048], P('dp'), may hold values from -6 to 6
- norm_gain: bfloat16 [2048], replicated, may hold values from 0.5 to 1.5
- norm_shift: bfloat16 [2048], replicated, may hold values from -3 to 3
- qkv_weight: bfloat16 [2048, 6144], P(None, 'tensor'), may hold values from -0.125 to 0.125
- qkv_bias: bfloat16 [6144], P('tensor'), may hold values from -3 to 3
- out_weight: bfloat16 [2048, 2048], P('tensor'), may hold values from -0.125 to 0.125
- out_bias: bfloat16 [2048], replicated, may hold values from -3 to 3
- pre_keys: bfloat16 [8, 1024, 2048], P('dp', None, 'tensor'), may hold values from -480 to 480
- pre_values: bfloat16 [8, 1024, 2048], P('dp', None, 'tensor'), may hold values from -6 to 6
- dec_keys: bfloat16 [16, 2048, 2048], P('dp', None, 'tensor'), may hold values from -480 to 480
- dec_values: bfloat16 [16, 2048, 2048], P('dp', None, 'tensor'), may hold values from -6 to 6
- prefix_lengths: int32 [8], P('dp'), may hold values from 0 to 1024, as said below
- cache_lengths: int32 [16], P('dp'), may hold values from 1 to 2048, as said below
- slot_of: int32 [16], replicated, may hold values from 0 to 15, each once
Outputs:
- pre_output: bfloat16 [8192, 2048], P(('dp', 'tensor'))
- dec_output: bfloat16 [16, 2048], P('dp')
Inputs may be any that keep to these rules, and one draw needn't show every extreme that they name: `slot_of`: each decode slot is used by exactly one decode request. `prefix_lengths`: the longest prefix equals 1024. `cache_lengths`: the longest decode cache equals 2048.
All inputs are finite; a program needn't handle non-finite values.
Results may differ from a plain program's by a relative error of at most 0.0049.
The roundings to bfloat16 on the way count: a program that leaves them out, or rounds other values in their place, can miss the bound.
Values may be sent and summed in bfloat16 or wider, within the bound.
No kernel may reach another device: no remote copies, remote signals or barrier semaphores. Data moves between devices by JAX's collectives and lax.ppermute only.
A program may use at most 128 MiB of HBM per device.

v0:
```python
import math
import jax
import jax.numpy as jnp
from jax import lax
from jax.sharding import PartitionSpec as P

H = 16
HD = 128
EPSILON = 1e-05


def normalize(values, norm_gain, norm_shift):
    values = values.astype(jnp.float32)
    center = values - jnp.mean(values, axis=-1, keepdims=True)
    spread = jnp.mean(center * center, axis=-1, keepdims=True)
    scaled = center * lax.rsqrt(spread + EPSILON)
    return (scaled * norm_gain.astype(jnp.float32) + norm_shift.astype(jnp.float32)).astype(
        jnp.bfloat16
    )


def alibi_slopes(first_head, head_count, total_heads):
    head_ids = (first_head + jnp.arange(head_count, dtype=jnp.int32)).astype(jnp.float32)
    return jnp.exp2(-8.0 * (head_ids + 1.0) / total_heads)


def prefill_attention(merged_rows, cache_keys, cache_values, prefix, slopes):
    queries = merged_rows[:, :, 0]
    new_keys = merged_rows[:, :, 1]
    new_values = merged_rows[:, :, 2]
    group_size = merged_rows.shape[0]
    cache_size = cache_keys.shape[0]
    factor = 1.0 / math.sqrt(merged_rows.shape[-1])
    query_pos = prefix + jnp.arange(group_size, dtype=jnp.int32)
    cache_pos = jnp.arange(cache_size, dtype=jnp.int32)
    cache_dist = (query_pos[:, None] - cache_pos[None, :]).astype(jnp.float32)
    new_dist = (query_pos[:, None] - query_pos[None, :]).astype(jnp.float32)
    cache_scores = (
        jnp.einsum("qhd,khd->hqk", queries, cache_keys, preferred_element_type=jnp.float32) * factor
    )
    cache_scores = cache_scores - slopes[:, None, None] * cache_dist[None]
    cache_scores = jnp.where((cache_pos < prefix)[None, None, :], cache_scores, -jnp.inf)
    new_scores = (
        jnp.einsum("qhd,khd->hqk", queries, new_keys, preferred_element_type=jnp.float32) * factor
    )
    new_scores = new_scores - slopes[:, None, None] * new_dist[None]
    causal = (
        jnp.arange(group_size, dtype=jnp.int32)[None, :]
        <= jnp.arange(group_size, dtype=jnp.int32)[:, None]
    )
    new_scores = jnp.where(causal[None], new_scores, -jnp.inf)
    highest = jnp.maximum(
        jnp.max(cache_scores, axis=-1, keepdims=True), jnp.max(new_scores, axis=-1, keepdims=True)
    )
    cache_exp = jnp.exp(cache_scores - highest)
    new_exp = jnp.exp(new_scores - highest)
    denominator = jnp.sum(cache_exp, axis=-1, keepdims=True) + jnp.sum(
        new_exp, axis=-1, keepdims=True
    )
    cache_probs = (cache_exp / denominator).astype(jnp.bfloat16)
    new_probs = (new_exp / denominator).astype(jnp.bfloat16)
    context = jnp.einsum(
        "hqk,khd->qhd", cache_probs, cache_values, preferred_element_type=jnp.float32
    )
    context = context + jnp.einsum(
        "hqk,khd->qhd", new_probs, new_values, preferred_element_type=jnp.float32
    )
    return context.astype(jnp.bfloat16).reshape(group_size, -1)


def decode_attention(query_row, new_key, new_value, cache_keys, cache_values, length, slopes):
    factor = 1.0 / math.sqrt(query_row.shape[-1])
    cache_pos = jnp.arange(cache_keys.shape[0], dtype=jnp.int32)
    distance = (length - cache_pos).astype(jnp.float32)
    cache_scores = (
        jnp.einsum("hd,khd->hk", query_row, cache_keys, preferred_element_type=jnp.float32) * factor
    )
    cache_scores = cache_scores - slopes[:, None] * distance[None, :]
    cache_scores = jnp.where((cache_pos < length)[None, :], cache_scores, -jnp.inf)
    own_score = (
        jnp.einsum("hd,hd->h", query_row, new_key, preferred_element_type=jnp.float32)[:, None]
        * factor
    )
    highest = jnp.maximum(jnp.max(cache_scores, axis=-1, keepdims=True), own_score)
    cache_exp = jnp.exp(cache_scores - highest)
    own_exp = jnp.exp(own_score - highest)
    denominator = jnp.sum(cache_exp, axis=-1, keepdims=True) + own_exp
    cache_probs = (cache_exp / denominator).astype(jnp.bfloat16)
    own_prob = (own_exp / denominator).astype(jnp.bfloat16)
    context = jnp.einsum(
        "hk,khd->hd", cache_probs, cache_values, preferred_element_type=jnp.float32
    )
    context = context + own_prob.astype(jnp.float32) * new_value.astype(jnp.float32)
    return context.astype(jnp.bfloat16).reshape(-1)


def per_device(
    pre_hidden,
    dec_hidden,
    norm_gain,
    norm_shift,
    qkv_weight,
    qkv_bias,
    out_weight,
    out_bias,
    pre_keys,
    pre_values,
    dec_keys,
    dec_values,
    prefix_lengths,
    cache_lengths,
    slot_of,
):
    head_size = HD
    local_heads = qkv_weight.shape[1] // (3 * head_size)
    slopes = alibi_slopes(lax.axis_index("tensor") * local_heads, local_heads, H)
    bias_sum = out_bias.astype(jnp.float32)
    normed = normalize(pre_hidden, norm_gain, norm_shift)
    product = jnp.dot(
        lax.all_gather(normed, "tensor", axis=0, tiled=True),
        qkv_weight,
        preferred_element_type=jnp.float32,
    )
    merged_rows = (product + qkv_bias.astype(jnp.float32)).astype(jnp.bfloat16)
    group_size = merged_rows.shape[0]
    merged_rows = merged_rows.reshape(group_size, local_heads, 3, head_size)
    cache_size = pre_keys.shape[1]
    context = prefill_attention(
        merged_rows,
        pre_keys[0].reshape(cache_size, local_heads, head_size),
        pre_values[0].reshape(cache_size, local_heads, head_size),
        prefix_lengths[0],
        slopes,
    )
    summed = lax.psum_scatter(
        jnp.dot(context, out_weight, preferred_element_type=jnp.float32),
        "tensor",
        scatter_dimension=0,
        tiled=True,
    )
    pre_output = (summed + bias_sum + pre_hidden.astype(jnp.float32)).astype(jnp.bfloat16)
    slot_count = dec_hidden.shape[0]
    request_count = slot_of.shape[0]
    first_slot = lax.axis_index("dp") * slot_count
    slot_ids = first_slot + jnp.arange(slot_count, dtype=jnp.int32)
    slot_pick = (slot_of[None, :] == slot_ids[:, None]).astype(jnp.bfloat16)
    own_slots = lax.dynamic_slice_in_dim(slot_of, first_slot, slot_count)
    send_pick = (jnp.arange(request_count, dtype=jnp.int32)[:, None] == own_slots[None, :]).astype(
        jnp.bfloat16
    )
    gathered = lax.all_gather(dec_hidden, "dp", axis=0, tiled=True)
    arrived = jnp.dot(slot_pick, gathered, preferred_element_type=jnp.float32).astype(jnp.bfloat16)
    normed_slots = normalize(arrived, norm_gain, norm_shift)
    merged_slots = (
        jnp.dot(normed_slots, qkv_weight, preferred_element_type=jnp.float32)
        + qkv_bias.astype(jnp.float32)
    ).astype(jnp.bfloat16)
    merged_slots = merged_slots.reshape(slot_count, local_heads, 3, head_size)
    dec_cache = dec_keys.shape[1]
    slot_context = jax.vmap(decode_attention, in_axes=(0, 0, 0, 0, 0, 0, None))(
        merged_slots[:, :, 0],
        merged_slots[:, :, 1],
        merged_slots[:, :, 2],
        dec_keys.reshape(slot_count, dec_cache, local_heads, head_size),
        dec_values.reshape(slot_count, dec_cache, local_heads, head_size),
        cache_lengths,
        slopes,
    )
    slot_partial = jnp.dot(slot_context, out_weight, preferred_element_type=jnp.float32)
    slot_summed = lax.psum(slot_partial, "tensor")
    slot_rows = (slot_summed + bias_sum + arrived.astype(jnp.float32)).astype(jnp.bfloat16)
    everything = lax.all_gather(slot_rows, "dp", axis=0, tiled=True)
    dec_output = jnp.dot(send_pick.T, everything, preferred_element_type=jnp.float32).astype(
        jnp.bfloat16
    )
    return (pre_output, dec_output)


def solution(mesh):
    placed = (
        P(("dp", "tensor"), None),
        P("dp", None),
        P(),
        P(),
        P(None, "tensor"),
        P("tensor"),
        P("tensor", None),
        P(),
        P("dp", None, "tensor"),
        P("dp", None, "tensor"),
        P("dp", None, "tensor"),
        P("dp", None, "tensor"),
        P("dp"),
        P("dp"),
        P(),
    )
    return jax.shard_map(
        per_device,
        mesh=mesh,
        in_specs=placed,
        out_specs=(P(("dp", "tensor"), None), P("dp", None)),
        check_vma=False,
    )
```

profile of v0, /device:TPU:0, one launch (start us, length us, event | category | flops | bytes accessed | tf_op | source)
XLA Modules:
  0.0 207.5 jit_solution(10675507170763093559)
XLA Ops:
  7.2 0.8 convert_element_type.111
  8.8 1.4 convert_reduce_fusion
  10.2 1.6 fusion.11
  11.9 2.8 %fusion.14 = bf16[256,2048]{1,0:T(8,128)(2,1)} fusion(bf16[256,2048]{1,0:T(8,128)(2,1)} %param.15, f32[2048]{0:T(1024)S(1)} %convert_element_type.112, f32[2048]{0:T(1024)S(1)} %convert_element_type.111, f32[256]{0:T(256)S(1)} %add_rsqrt_fusion, f32[256]{0:T(256)S(1)} %broadcast_multiply_fusion), kind=kLoop, calls=%fused_computation.30 | loop fusion | flops 3145728 | bytes 2115584 | tf_op jit(solution)/shard_map/convert_element_type | solution.py:17
  15.4 1.3 reshape_squeeze.6
  16.7 2.3 %copy.59 = bf16[1,1024,512]{1,2,0:T(8,128)(2,1)} copy(bf16[1,1024,512]{2,1,0:T(8,128)(2,1)} %param.24) | data formatting | bytes 2097152 | tf_op jit(solution)/shard_map/reshape;squeeze | solution.py:131
  19.0 1.3 iota_compare_fusion
  20.3 3.7 %subtract_convert_fusion = (f32[1024,1024]{0,1:T(8,128)}, f32[1024,1024]{0,1:T(8,128)}) fusion(s32[1024]{0:T(1024)S(1)} %iota_add_fusion), kind=kLoop, calls=%fused_computation.14 | loop fusion | flops 4194304 | bytes 8392704 | tf_op jit(solution)/shard_map/convert_element_type | solution.py:37
  24.0 28.0 %all-gather.4.cloned.1.call-done = bf16[1024,2048]{1,0:T(8,128)(2,1)} async-done(((bf16[256,2048]{1,0:T(8,128)(2,1)}), bf16[1024,2048]{1,0:T(8,128)(2,1)}) %all-gather.4.cloned.1.call-update) | async-done | bytes 4194320 | tf_op jit(solution)/shard_map/all_gather | solution.py:120
  52.0 11.2 %add_convert_fusion = bf16[1024,1536]{1,0:T(8,128)(2,1)} fusion(bf16[1024,2048]{1,0:T(8,128)(2,1)} %all-gather.4.cloned.1.call-done, bf16[2048,1536]{1,0:T(8,128)(2,1)} %param.19, f32[1536]{0:T(1024)S(1)} %convert_element_type.114), kind=kOutput, calls=%fused_computation.10 | convolution fusion | flops 6445596672 | bytes 13637632 | tf_op jit(solution)/shard_map/dot_general | solution.py:119
  63.2 4.7 %copy.40 = bf16[1024,1536]{0,1:T(8,128)(2,1)} copy(bf16[1024,1536]{1,0:T(8,128)(2,1)} %add_convert_fusion) | data formatting | bytes 6291456 | tf_op jit(solution)/shard_map/convert_element_type | solution.py:124
  67.9 10.8 %fusion.44 = (f32[4,1024]{1,0:T(4,128)S(1)}, f32[4,1024,1024]{1,2,0:T(8,128)}) fusion(f32[1024,1024]{0,1:T(8,128)} %get-tuple-element.9, f32[4]{0:T(128)S(1)} %multiply_exponential_fusion, bf16[1024,4,3,128]{0,3,2,1:T(8,128)(2,1)} %bitcast.79, pred[1024,1024]{0,1:T(8,128)(4,1)} %iota_compare_fusion), kind=kOutput, calls=%fused_computation.86 | convolution fusion | flops 1094709248 | bytes 24133648 | tf_op jit(solution)/shard_map/qhd,khd->hqk/dot_general | solution.py:44
  78.7 3.7 %fusion.43 = (f32[4,1024]{1,0:T(4,128)S(1)}, f32[4,1024,1024]{1,2,0:T(8,128)S(1)}) fusion(f32[1024,1024]{0,1:T(8,128)S(1)} %copy-done.1, f32[4]{0:T(128)S(1)} %multiply_exponential_fusion, bf16[1024,4,3,128]{0,3,2,1:T(8,128)(2,1)S(1)} %bitcast.80, bf16[1024,4,128]{2,1,0:T(4,128)(2,1)S(1)} %reshape_squeeze.6, pred[1024]{0:T(1024)(128)(4,1)S(1)} %iota_compare_fusion.4), kind=kOutput, calls=%fused_computation.85 | convolution fusion | flops 1094709248 | bytes 23086592 | tf_op jit(solution)/shard_map/qhd,khd->hqk/dot_general | solution.py:39
  82.5 8.4 %fusion.1 = (f32[4,1024]{1,0:T(4,128)S(1)}, f32[4,1024]{1,0:T(4,128)S(1)}) fusion(f32[4,1024,1024]{1,2,0:T(8,128)} %get-tuple-element.16, f32[4,1024]{1,0:T(4,128)S(1)} %max.12, f32[4,1024,1024]{1,2,0:T(8,128)S(1)} %get-tuple-element.14), kind=kLoop, calls=%fused_computation.7 | loop fusion | flops 16769024 | bytes 33603584 | tf_op jit(solution)/shard_map/reduce_sum | solution.py:57
  90.9 3.7 %fusion.2 = f32[4,1024,128]{1,2,0:T(8,128)S(1)} fusion(bf16[1024,4,128]{0,2,1:T(8,128)(2,1)S(1)} %bitcast.82, f32[4,1024,1024]{1,2,0:T(8,128)S(1)} %get-tuple-element.14, f32[4,1024]{1,0:T(4,128)S(1)} %add.155, f32[4,1024]{1,0:T(4,128)S(1)} %max.12), kind=kOutput, calls=%fused_computation.8 | convolution fusion | flops 1086324736 | bytes 19955712 | tf_op jit(solution)/shard_map/hqk,khd->qhd/dot_general | solution.py:62
  94.6 7.7 %fusion.16 = bf16[1024,4,128]{0,2,1:T(8,128)(2,1)S(1)} fusion(f32[4,1024,128]{1,2,0:T(8,128)S(1)} %fusion.2, f32[4,1024,1024]{1,2,0:T(8,128)} %get-tuple-element.16, f32[4,1024]{1,0:T(4,128)S(1)} %add.155, f32[4,1024]{1,0:T(4,128)S(1)} %max.12, bf16[1024,4,3,128]{0,3,2,1:T(8,128)(2,1)S(1)} %bitcast.81), kind=kOutput, calls=%fused_computation.33 | convolution fusion | flops 1087373312 | bytes 21004288 | tf_op jit(solution)/shard_map/hqk,khd->qhd/dot_general | solution.py:65
  102.3 5.6 %fusion.46 = f32[1024,2048]{1,0:T(8,128)} fusion(bf16[1024,512]{0,1:T(8,128)(2,1)S(1)} %bitcast.86, bf16[512,2048]{1,0:T(8,128)(2,1)S(1)} %copy-done), kind=kOutput, calls=%fused_computation.88 | convolution fusion | flops 2147483648 | bytes 11534336 | tf_op jit(solution)/shard_map/dot_general | solution.py:136
  108.6 30.6 %all-gather = bf16[8,2,2048]{2,1,0:T(2,128)(2,1)S(1)} all-gather(bf16[1,2,2048]{2,1,0:T(2,128)(2,1)S(1)} %bitcast.84), channel_id=1, replica_groups=mesh['dp'=8,'tensor'=4] {'dp'}, dimensions={0}, use_global_device_ids=true | all-gather | bytes 73728 | tf_op jit(solution)/shard_map/all_gather | solution.py:151
  139.7 4.0 %fusion.9 = bf16[2,1536]{1,0:T(2,128)(2,1)S(1)} fusion(bf16[2048,1536]{1,0:T(8,128)(2,1)} %param.19, f32[2,2048]{1,0:T(2,128)S(1)} %get-tuple-element.18, f32[2]{0:T(128)S(1)} %add_rsqrt_fusion.1, f32[2]{0:T(128)S(1)} %broadcast_multiply_fusion.1, f32[2048]{0:T(1024)S(1)} %convert_element_type.112, f32[2048]{0:T(1024)S(1)} %convert_element_type.111, ...), kind=kOutput, calls=%fused_computation.23 | convolution fusion | flops 12609536 | bytes 6336528 | tf_op jit(solution)/shard_map/dot_general | solution.py:155
  143.8 6.3 %copy.60 = bf16[2,2048,512]{1,2,0:T(8,128)(2,1)} copy(bf16[2,2048,512]{2,1,0:T(8,128)(2,1)} %param.25) | data formatting | bytes 8388608 | tf_op jit(solution)/shard_map/reshape | solution.py:164
  150.2 3.2 %fusion.28 = f32[2,4,1,2048]{3,2,1,0:T(1,128)S(1)} fusion(bf16[2,2048,4,128]{1,3,2,0:T(8,128)(2,1)} %bitcast.78, bf16[2,4,3,128]{3,2,1,0:T(4,128)(2,1)S(1)} %reshape.204), kind=kOutput, calls=%fused_computation.59 | convolution fusion | flops 4194304 | bytes 4263936 | tf_op jit(solution)/shard_map/vmap(hd,khd->hk)/dot_general | solution.py:76
  155.2 11.1 %psum.7 = f32[2,2048]{1,0:T(2,128)S(1)} all-reduce(f32[2,2048]{1,0:T(2,128)S(1)} %fusion.32), channel_id=1, replica_groups=mesh['dp'=8,'tensor'=4] {'tensor'}, use_global_device_ids=true, to_apply=%region_11.12 | all-reduce | flops 4096 | bytes 32768 | tf_op jit(solution)/shard_map/psum | solution.py:170
  166.4 30.5 %all-gather.1 = bf16[8,2,2048]{2,1,0:T(2,128)(2,1)S(1)} all-gather(bf16[1,2,2048]{2,1,0:T(2,128)(2,1)S(1)} %fusion.24), channel_id=1, replica_groups=mesh['dp'=8,'tensor'=4] {'dp'}, dimensions={0}, use_global_device_ids=true | all-gather | bytes 73728 | tf_op jit(solution)/shard_map/all_gather | solution.py:172
  197.8 2.9 %fusion.15 = bf16[256,2048]{1,0:T(8,128)(2,1)} fusion(bf16[256,2048]{1,0:T(8,128)(2,1)S(1)} %copy-done.2, f32[256,2048]{1,0:T(8,128)} %reduce-scatter.2.cloned.1.call-done, f32[2048]{0:T(1024)S(1)} %convert_element_type.122), kind=kLoop, calls=%fused_computation.31 | loop fusion | flops 2097152 | bytes 4202496 | tf_op jit(solution)/shard_map/convert_element_type | solution.py:141
  (60 shorter events, 5.0 us)
Async XLA Ops:
  7.2 95.1 %copy-start = (bf16[512,2048]{1,0:T(8,128)(2,1)S(1)}, bf16[512,2048]{1,0:T(8,128)(2,1)}, u32[]{:S(2)}) copy-start(bf16[512,2048]{1,0:T(8,128)(2,1)} %param.21) | copy-start | bytes 6291460
  7.2 7.5 %copy-start.6 = (bf16[1536]{0:T(1024)(128)(2,1)S(1)}, bf16[1536]{0:T(1024)(128)(2,1)}, u32[]{:S(2)}) copy-start(bf16[1536]{0:T(1024)(128)(2,1)} %param.20) | copy-start | bytes 9220
  7.2 44.8 %all-gather.4.cloned.1.call-start = ((), (), s32[]{:S(2)}) async-start(), calls=%async_computation.1 | async-start | bytes 5242880 | tf_op jit(solution)/shard_map/all_gather | solution.py:120
  14.6 183.1 %reduce-scatter.2.cloned.1.call-start = ((), (), s32[]{:S(2)}) async-start(), calls=%async_computation.2 | async-start | bytes 10485760 | tf_op jit(solution)/shard_map/reduce_scatter | solution.py:135
  67.9 10.9 %copy-start.1 = (f32[1024,1024]{0,1:T(8,128)S(1)}, f32[1024,1024]{0,1:T(8,128)}, u32[]{:S(2)}) copy-start(f32[1024,1024]{0,1:T(8,128)} %get-tuple-element.10) | copy-start | bytes 12582916
  67.9 10.9 %copy-start.3 = (bf16[1024,1536]{0,1:T(8,128)(2,1)S(1)}, bf16[1024,1536]{0,1:T(8,128)(2,1)}, u32[]{:S(2)}) copy-start(bf16[1024,1536]{0,1:T(8,128)(2,1)} %copy.40) | copy-start | bytes 9437188
  82.4 8.4 %copy-start.4 = (bf16[1,1024,512]{1,2,0:T(8,128)(2,1)S(1)}, bf16[1,1024,512]{1,2,0:T(8,128)(2,1)}, u32[]{:S(2)}) copy-start(bf16[1,1024,512]{1,2,0:T(8,128)(2,1)} %copy.59) | copy-start | bytes 3145732
  107.9 0.7 copy-start.7
  107.9 0.7 copy-start.5
  107.9 31.3 %copy-start.10 = (s32[16]{0:T(128)S(1)}, s32[16]{0:T(128)}, u32[]{:S(2)}) copy-start(s32[16]{0:T(128)} %param.29) | copy-start | bytes 196
  150.1 3.3 %copy-start.8 = (s32[2]{0:T(128)S(1)}, s32[2]{0:T(128)}, u32[]{:S(2)}) copy-start(s32[2]{0:T(128)} %param.28) | copy-start | bytes 28
  150.1 4.0 %copy-start.9 = (bf16[2,2048,512]{2,1,0:T(8,128)(2,1)S(1)}, bf16[2,2048,512]{2,1,0:T(8,128)(2,1)}, u32[]{:S(2)}) copy-start(bf16[2,2048,512]{2,1,0:T(8,128)(2,1)} %param.26) | copy-start | bytes 12582916
  153.4 44.4 %copy-start.2 = (bf16[256,2048]{1,0:T(8,128)(2,1)S(1)}, bf16[256,2048]{1,0:T(8,128)(2,1)}, u32[]{:S(2)}) copy-start(bf16[256,2048]{1,0:T(8,128)(2,1)} %param.15) | copy-start | bytes 3145732
Sparse Core Ops, SparseCore 0:
  14.8 37.1 all-gather.3
  108.0 71.9 reduce-scatter.1
where the time goes:
time: 208 us; the launch traced here: 207 us
  blocking collectives  72.2 us (35%)
  matrix products  52.1 us (25%)
  waiting for transfers between devices  28 us (13%)
  other arithmetic  24.7 us (12%)
  local copies, waits for them, and re-layouts  15.5 us (7%)
  between operations  14.9 us (7%)
    all_gather x1, blocking collectives, per_device(): gathered = lax.all_gather(dec_hidden, 'dp', axis=0, tiled=True)  30.6 us
    all_gather x1, blocking collectives, per_device(): everything = lax.all_gather(slot_rows, 'dp', axis=0, tiled=True)  30.5 us
    all_gather x1, waiting for transfers between devices, per_device(): lax.all_gather(normed, 'tensor', axis=0, tiled=True)  28 us
    dot_general x1, matrix products, per_device(): jnp.dot(lax.all_gather(normed, 'tensor', axis=0, tiled=True), qkv_weight,...  11.2 us
    psum x1, blocking collectives, per_device(): slot_summed = lax.psum(slot_partial, 'tensor')  11.1 us
    dot_general x1, matrix products, prefill_attention(): jnp.einsum('qhd,khd->hqk', queries, new_keys, preferred_element_type=jnp....  10.8 us
    reduce_sum x1, other arithmetic, prefill_attention(): jnp.sum(new_exp, axis=-1, keepdims=True)  8.4 us
    dot_general x1, matrix products, prefill_attention(): jnp.einsum('hqk,khd->qhd', new_probs, new_values, preferred_element_type=...  7.69 us
  transfers between devices with their start and end apart: 2, of which 1 were waited for; matrix products, arithmetic and copies ran while one was open for 12% of the time, Pallas kernels for 0%

commit v1 on v0

--- a/solution.py
+++ b/solution.py
@@ -167,7 +167,8 @@
         slopes,
     )
     slot_partial = jnp.dot(slot_context, out_weight, preferred_element_type=jnp.float32)
-    slot_summed = lax.psum(slot_partial, "tensor")
+    pieces = lax.all_gather(slot_partial, "tensor", axis=0, tiled=False)
+    slot_summed = pieces.sum(axis=0)
     slot_rows = (slot_summed + bias_sum + arrived.astype(jnp.float32)).astype(jnp.bfloat16)
     everything = lax.all_gather(slot_rows, "dp", axis=0, tiled=True)
     dec_output = jnp.dot(send_pick.T, everything, preferred_element_type=jnp.float32).astype(

time: 208 us -> 203 us (0.976)
  blocking collectives: 72.2 us -> 66.6 us
    psum x1 -> x0, blocking collectives: 11.1 us -> none  [per_device(): slot_summed = lax.psum(slot_partial, 'tensor')]
    all_gather x0 -> x1, blocking collectives: none -> 5.56 us  [per_device(): pieces = lax.all_gather(slot_partial, 'tensor', axis=0, tiled=False)]
  transfers between devices with their start and end apart: 2 -> 2, of which waited for: 1 -> 1; matrix products, arithmetic and copies ran while one was open for 12% -> 13% of each run, Pallas kernels for 0% -> 0%
where the time goes in v1:
time: 203 us; the launch traced here: 202 us
  blocking collectives  66.6 us (33%)
  matrix products  52.1 us (26%)
  waiting for transfers between devices  28 us (14%)
  other arithmetic  24.7 us (12%)
  local copies, waits for them, and re-layouts  15.5 us (8%)
  between operations  14.9 us (7%)
    all_gather x1, blocking collectives, per_device(): gathered = lax.all_gather(dec_hidden, 'dp', axis=0, tiled=True)  30.6 us
    all_gather x1, blocking collectives, per_device(): everything = lax.all_gather(slot_rows, 'dp', axis=0, tiled=True)  30.5 us
    all_gather x1, waiting for transfers between devices, per_device(): lax.all_gather(normed, 'tensor', axis=0, tiled=True)  28 us
    dot_general x1, matrix products, per_device(): jnp.dot(lax.all_gather(normed, 'tensor', axis=0, tiled=True), qkv_weight,...  11.2 us
    dot_general x1, matrix products, prefill_attention(): jnp.einsum('qhd,khd->hqk', queries, new_keys, preferred_element_type=jnp....  10.8 us
    reduce_sum x1, other arithmetic, prefill_attention(): jnp.sum(new_exp, axis=-1, keepdims=True)  8.4 us
    dot_general x1, matrix products, prefill_attention(): jnp.einsum('hqk,khd->qhd', new_probs, new_values, preferred_element_type=...  7.69 us
    reshape x1, local copies, waits for them, and re-layouts, per_device(): dec_keys.reshape(slot_count, dec_cache, local_heads, head_size)  6.31 us
  transfers between devices with their start and end apart: 2, of which 1 were waited for; matrix products, arithmetic and copies ran while one was open for 13% of the time, Pallas kernels for 0%

profile of v1, /device:TPU:0, one launch (start us, length us, event | category | flops | bytes accessed | tf_op | source)
XLA Modules:
  0.0 202.0 jit_solution(16831610453844583385)
XLA Ops:
  7.2 0.8 convert_element_type.111
  8.8 1.4 convert_reduce_fusion
  10.2 1.6 fusion.11
  11.9 2.8 %fusion.14 = bf16[256,2048]{1,0:T(8,128)(2,1)} fusion(bf16[256,2048]{1,0:T(8,128)(2,1)} %param.15, f32[2048]{0:T(1024)S(1)} %convert_element_type.112, f32[2048]{0:T(1024)S(1)} %convert_element_type.111, f32[256]{0:T(256)S(1)} %add_rsqrt_fusion, f32[256]{0:T(256)S(1)} %broadcast_multiply_fusion), kind=kLoop, calls=%fused_computation.31 | loop fusion | flops 3145728 | bytes 2115584 | tf_op jit(solution)/shard_map/convert_element_type | solution.py:17
  15.4 1.3 reshape_squeeze.6
  16.7 2.3 %copy.59 = bf16[1,1024,512]{1,2,0:T(8,128)(2,1)} copy(bf16[1,1024,512]{2,1,0:T(8,128)(2,1)} %param.24) | data formatting | bytes 2097152 | tf_op jit(solution)/shard_map/reshape;squeeze | solution.py:131
  19.0 1.3 iota_compare_fusion
  20.3 3.7 %subtract_convert_fusion = (f32[1024,1024]{0,1:T(8,128)}, f32[1024,1024]{0,1:T(8,128)}) fusion(s32[1024]{0:T(1024)S(1)} %iota_add_fusion), kind=kLoop, calls=%fused_computation.14 | loop fusion | flops 4194304 | bytes 8392704 | tf_op jit(solution)/shard_map/convert_element_type | solution.py:37
  24.0 28.0 %all-gather.6.cloned.1.call-done = bf16[1024,2048]{1,0:T(8,128)(2,1)} async-done(((bf16[256,2048]{1,0:T(8,128)(2,1)}), bf16[1024,2048]{1,0:T(8,128)(2,1)}) %all-gather.6.cloned.1.call-update) | async-done | bytes 4194320 | tf_op jit(solution)/shard_map/all_gather | solution.py:120
  52.0 11.2 %add_convert_fusion = bf16[1024,1536]{1,0:T(8,128)(2,1)} fusion(bf16[1024,2048]{1,0:T(8,128)(2,1)} %all-gather.6.cloned.1.call-done, bf16[2048,1536]{1,0:T(8,128)(2,1)} %param.19, f32[1536]{0:T(1024)S(1)} %convert_element_type.114), kind=kOutput, calls=%fused_computation.10 | convolution fusion | flops 6445596672 | bytes 13637632 | tf_op jit(solution)/shard_map/dot_general | solution.py:119
  63.2 4.7 %copy.40 = bf16[1024,1536]{0,1:T(8,128)(2,1)} copy(bf16[1024,1536]{1,0:T(8,128)(2,1)} %add_convert_fusion) | data formatting | bytes 6291456 | tf_op jit(solution)/shard_map/convert_element_type | solution.py:124
  67.9 10.8 %fusion.43 = (f32[4,1024]{1,0:T(4,128)S(1)}, f32[4,1024,1024]{1,2,0:T(8,128)}) fusion(f32[1024,1024]{0,1:T(8,128)} %get-tuple-element.9, f32[4]{0:T(128)S(1)} %multiply_exponential_fusion, bf16[1024,4,3,128]{0,3,2,1:T(8,128)(2,1)} %bitcast.81, pred[1024,1024]{0,1:T(8,128)(4,1)} %iota_compare_fusion), kind=kOutput, calls=%fused_computation.86 | convolution fusion | flops 1094709248 | bytes 24133648 | tf_op jit(solution)/shard_map/qhd,khd->hqk/dot_general | solution.py:44
  78.7 3.7 %fusion.42 = (f32[4,1024]{1,0:T(4,128)S(1)}, f32[4,1024,1024]{1,2,0:T(8,128)S(1)}) fusion(f32[1024,1024]{0,1:T(8,128)S(1)} %copy-done.1, f32[4]{0:T(128)S(1)} %multiply_exponential_fusion, bf16[1024,4,3,128]{0,3,2,1:T(8,128)(2,1)S(1)} %bitcast.82, bf16[1024,4,128]{2,1,0:T(4,128)(2,1)S(1)} %reshape_squeeze.6, pred[1024]{0:T(1024)(128)(4,1)S(1)} %iota_compare_fusion.4), kind=kOutput, calls=%fused_computation.85 | convolution fusion | flops 1094709248 | bytes 23086592 | tf_op jit(solution)/shard_map/qhd,khd->hqk/dot_general | solution.py:39
  82.5 8.4 %fusion.1 = (f32[4,1024]{1,0:T(4,128)S(1)}, f32[4,1024]{1,0:T(4,128)S(1)}) fusion(f32[4,1024,1024]{1,2,0:T(8,128)} %get-tuple-element.16, f32[4,1024]{1,0:T(4,128)S(1)} %max.12, f32[4,1024,1024]{1,2,0:T(8,128)S(1)} %get-tuple-element.14), kind=kLoop, calls=%fused_computation.7 | loop fusion | flops 16769024 | bytes 33603584 | tf_op jit(solution)/shard_map/reduce_sum | solution.py:57
  90.9 3.7 %fusion.2 = f32[4,1024,128]{1,2,0:T(8,128)S(1)} fusion(bf16[1024,4,128]{0,2,1:T(8,128)(2,1)S(1)} %bitcast.84, f32[4,1024,1024]{1,2,0:T(8,128)S(1)} %get-tuple-element.14, f32[4,1024]{1,0:T(4,128)S(1)} %add.153, f32[4,1024]{1,0:T(4,128)S(1)} %max.12), kind=kOutput, calls=%fused_computation.8 | convolution fusion | flops 1086324736 | bytes 19955712 | tf_op jit(solution)/shard_map/hqk,khd->qhd/dot_general | solution.py:62
  94.6 7.7 %fusion.16 = bf16[1024,4,128]{0,2,1:T(8,128)(2,1)S(1)} fusion(f32[4,1024,128]{1,2,0:T(8,128)S(1)} %fusion.2, f32[4,1024,1024]{1,2,0:T(8,128)} %get-tuple-element.16, f32[4,1024]{1,0:T(4,128)S(1)} %add.153, f32[4,1024]{1,0:T(4,128)S(1)} %max.12, bf16[1024,4,3,128]{0,3,2,1:T(8,128)(2,1)S(1)} %bitcast.83), kind=kOutput, calls=%fused_computation.34 | convolution fusion | flops 1087373312 | bytes 21004288 | tf_op jit(solution)/shard_map/hqk,khd->qhd/dot_general | solution.py:65
  102.3 5.6 %fusion.45 = f32[1024,2048]{1,0:T(8,128)} fusion(bf16[1024,512]{0,1:T(8,128)(2,1)S(1)} %bitcast.88, bf16[512,2048]{1,0:T(8,128)(2,1)S(1)} %copy-done), kind=kOutput, calls=%fused_computation.88 | convolution fusion | flops 2147483648 | bytes 11534336 | tf_op jit(solution)/shard_map/dot_general | solution.py:136
  108.6 30.6 %all-gather.1 = bf16[8,2,2048]{2,1,0:T(2,128)(2,1)S(1)} all-gather(bf16[1,2,2048]{2,1,0:T(2,128)(2,1)S(1)} %bitcast.86), channel_id=1, replica_groups=mesh['dp'=8,'tensor'=4] {'dp'}, dimensions={0}, use_global_device_ids=true | all-gather | bytes 73728 | tf_op jit(solution)/shard_map/all_gather | solution.py:151
  139.7 4.0 %fusion.9 = bf16[2,1536]{1,0:T(2,128)(2,1)S(1)} fusion(bf16[2048,1536]{1,0:T(8,128)(2,1)} %param.19, f32[2,2048]{1,0:T(2,128)S(1)} %get-tuple-element.18, f32[2]{0:T(128)S(1)} %add_rsqrt_fusion.1, f32[2]{0:T(128)S(1)} %broadcast_multiply_fusion.1, f32[2048]{0:T(1024)S(1)} %convert_element_type.112, f32[2048]{0:T(1024)S(1)} %convert_element_type.111, ...), kind=kOutput, calls=%fused_computation.24 | convolution fusion | flops 12609536 | bytes 6336528 | tf_op jit(solution)/shard_map/dot_general | solution.py:155
  143.8 6.3 %copy.60 = bf16[2,2048,512]{1,2,0:T(8,128)(2,1)} copy(bf16[2,2048,512]{2,1,0:T(8,128)(2,1)} %param.25) | data formatting | bytes 8388608 | tf_op jit(solution)/shard_map/reshape | solution.py:164
  150.2 3.2 %fusion.28 = f32[2,4,1,2048]{3,2,1,0:T(1,128)S(1)} fusion(bf16[2,2048,4,128]{1,3,2,0:T(8,128)(2,1)} %bitcast.80, bf16[2,4,3,128]{3,2,1,0:T(4,128)(2,1)S(1)} %reshape.204), kind=kOutput, calls=%fused_computation.60 | convolution fusion | flops 4194304 | bytes 4263936 | tf_op jit(solution)/shard_map/vmap(hd,khd->hk)/dot_general | solution.py:76
  155.2 5.6 %all-gather.2 = f32[4,2,2048]{2,1,0:T(2,128)S(1)} all-gather(f32[1,2,2048]{2,1,0:T(2,128)S(1)} %convolution_bitcast_fusion), channel_id=2, replica_groups=mesh['dp'=8,'tensor'=4] {'tensor'}, dimensions={0}, use_global_device_ids=true | all-gather | bytes 81920 | tf_op jit(solution)/shard_map/all_gather | solution.py:170
  160.8 30.5 %all-gather.3 = bf16[8,2,2048]{2,1,0:T(2,128)(2,1)S(1)} all-gather(bf16[1,2,2048]{2,1,0:T(2,128)(2,1)S(1)} %fusion.24), channel_id=1, replica_groups=mesh['dp'=8,'tensor'=4] {'dp'}, dimensions={0}, use_global_device_ids=true | all-gather | bytes 73728 | tf_op jit(solution)/shard_map/all_gather | solution.py:173
  192.2 2.9 %fusion.15 = bf16[256,2048]{1,0:T(8,128)(2,1)} fusion(bf16[256,2048]{1,0:T(8,128)(2,1)S(1)} %copy-done.2, f32[256,2048]{1,0:T(8,128)} %reduce-scatter.2.cloned.1.call-done, f32[2048]{0:T(1024)S(1)} %convert_element_type.122), kind=kLoop, calls=%fused_computation.32 | loop fusion | flops 2097152 | bytes 4202496 | tf_op jit(solution)/shard_map/convert_element_type | solution.py:141
  (61 shorter events, 5.0 us)
Async XLA Ops:
  7.2 95.1 %copy-start = (bf16[512,2048]{1,0:T(8,128)(2,1)S(1)}, bf16[512,2048]{1,0:T(8,128)(2,1)}, u32[]{:S(2)}) copy-start(bf16[512,2048]{1,0:T(8,128)(2,1)} %param.21) | copy-start | bytes 6291460
  7.2 7.5 %copy-start.6 = (bf16[1536]{0:T(1024)(128)(2,1)S(1)}, bf16[1536]{0:T(1024)(128)(2,1)}, u32[]{:S(2)}) copy-start(bf16[1536]{0:T(1024)(128)(2,1)} %param.20) | copy-start | bytes 9220
  7.2 44.8 %all-gather.6.cloned.1.call-start = ((), (), s32[]{:S(2)}) async-start(), calls=%async_computation.1 | async-start | bytes 5242880 | tf_op jit(solution)/shard_map/all_gather | solution.py:120
  14.6 177.6 %reduce-scatter.2.cloned.1.call-start = ((), (), s32[]{:S(2)}) async-start(), calls=%async_computation.2 | async-start | bytes 10485760 | tf_op jit(solution)/shard_map/reduce_scatter | solution.py:135
  67.9 10.9 %copy-start.1 = (f32[1024,1024]{0,1:T(8,128)S(1)}, f32[1024,1024]{0,1:T(8,128)}, u32[]{:S(2)}) copy-start(f32[1024,1024]{0,1:T(8,128)} %get-tuple-element.10) | copy-start | bytes 12582916
  67.9 10.9 %copy-start.3 = (bf16[1024,1536]{0,1:T(8,128)(2,1)S(1)}, bf16[1024,1536]{0,1:T(8,128)(2,1)}, u32[]{:S(2)}) copy-start(bf16[1024,1536]{0,1:T(8,128)(2,1)} %copy.40) | copy-start | bytes 9437188
  82.4 8.4 %copy-start.4 = (bf16[1,1024,512]{1,2,0:T(8,128)(2,1)S(1)}, bf16[1,1024,512]{1,2,0:T(8,128)(2,1)}, u32[]{:S(2)}) copy-start(bf16[1,1024,512]{1,2,0:T(8,128)(2,1)} %copy.59) | copy-start | bytes 3145732
  107.9 0.7 copy-start.7
  107.9 0.7 copy-start.5
  107.9 31.3 %copy-start.10 = (s32[16]{0:T(128)S(1)}, s32[16]{0:T(128)}, u32[]{:S(2)}) copy-start(s32[16]{0:T(128)} %param.29) | copy-start | bytes 196
  150.1 3.3 %copy-start.8 = (s32[2]{0:T(128)S(1)}, s32[2]{0:T(128)}, u32[]{:S(2)}) copy-start(s32[2]{0:T(128)} %param.28) | copy-start | bytes 28
  150.1 4.0 %copy-start.9 = (bf16[2,2048,512]{2,1,0:T(8,128)(2,1)S(1)}, bf16[2,2048,512]{2,1,0:T(8,128)(2,1)}, u32[]{:S(2)}) copy-start(bf16[2,2048,512]{2,1,0:T(8,128)(2,1)} %param.26) | copy-start | bytes 12582916
  153.4 38.8 %copy-start.2 = (bf16[256,2048]{1,0:T(8,128)(2,1)S(1)}, bf16[256,2048]{1,0:T(8,128)(2,1)}, u32[]{:S(2)}) copy-start(bf16[256,2048]{1,0:T(8,128)(2,1)} %param.15) | copy-start | bytes 3145732
Sparse Core Ops, SparseCore 0:
  14.8 37.1 all-gather.5
  108.0 72.0 reduce-scatter.1
